TPU v7x, 32 devices: a whole 2x2x4 slice. The times are simulated.
32 devices in a mesh: groups: 2 (over x), date: 8 (over z, y), row: 2 (over core).
Axes of the slice: x: 2, y: 2, z: 4, core: 2. Of those that a mesh axis runs over, the one named last changes fastest.
Arguments:
- scenes: bfloat16 [16, 4, 512, 1024], P(('groups', 'date'), None, 'row'), parts along dimension 0, may hold values from -6 to 6
- resample_taps: float32 [2, 4, 7], replicated, may hold values from 0 to 0.35
- clear_mask: int32 [16, 128, 8], P('groups', ('row', 'date')), parts along dimension 0, may hold values 0 or 1
Outputs:
- smooth_fine: bfloat16 [16, 4, 512, 1024], P('groups', None, ('row', 'date')), parts along dimension 0
- smooth_half: bfloat16 [16, 4, 256, 512], P('groups', None, ('row', 'date')), parts along dimension 0
- smooth_quarter: bfloat16 [16, 4, 128, 256], P('groups', None, ('row', 'date')), parts along dimension 0
There are 2 independent parts, one for each index of `groups`. A program takes and returns all parts, laid end to end along the dimension named above; an argument that names none is the same for every part. Nothing has to cross between parts.
Inputs may be any that keep to these rules, and one draw needn't show every extreme that they name: `clear_mask`: 1 marks a clear block, 0 a cloudy one.
All inputs are finite; a program needn't handle non-finite values.
Results may differ from a plain program's by a relative error of at most 0.005.
Values may be sent and summed in bfloat16 or wider, within the bound.
No kernel may reach another device: no remote copies, remote signals or barrier semaphores. Data moves between devices by JAX's collectives and lax.ppermute only.
A program may use at most 128 MiB of HBM per device.

v0:
```python
import math
import jax
import jax.numpy as jnp
from jax import lax
from jax.sharding import PartitionSpec as P

gap_weights = [math.exp(-((k - 4) ** 2) / 8.0) for k in range(9)]
savgol_coeffs = [c / 231.0 for c in [-21.0, 14.0, 39.0, 54.0, 59.0, 54.0, 39.0, 14.0, -21.0]]
pyramid_filter = [0.125, 0.375, 0.375, 0.125]


def padded(block, sides, width):
    for axis, dim in sides:
        count = lax.axis_size(axis)
        forward = [(i, i + 1) for i in range(count - 1)]
        backward = [(target, source) for source, target in forward]
        low = lax.ppermute(
            lax.slice_in_dim(block, block.shape[dim] - width, None, axis=dim), axis, forward
        )
        high = lax.ppermute(lax.slice_in_dim(block, 0, width, axis=dim), axis, backward)
        block = jnp.concatenate([low, block, high], axis=dim)
    return block


def valid_taps(values, taps, axis):
    count = values.shape[axis] - 6
    total = jnp.zeros(values.shape[:axis] + (count,) + values.shape[axis + 1 :], jnp.float32)
    for k in range(7):
        shape = [1] * values.ndim
        shape[-3] = taps.shape[0]
        total = total + taps[:, k].reshape(shape) * lax.slice_in_dim(values, k, k + count, 1, axis)
    return total


def column_resample(values, taps):
    width = values.shape[3]
    source = lax.broadcasted_iota(jnp.int32, (width, width), 0)
    target = lax.broadcasted_iota(jnp.int32, (width, width), 1)
    offset = source - target + 3
    table = jnp.zeros((taps.shape[0], width, width), jnp.float32)
    for k in range(7):
        table = table + taps[:, k][:, None, None] * (offset == k).astype(jnp.float32)[None]
    return jnp.einsum(
        "tbrc,bcd->tbrd", values.astype(jnp.float32), table, precision=lax.Precision.HIGHEST
    )


def halve_columns(values):
    width = values.shape[3]
    source = lax.broadcasted_iota(jnp.int32, (width, width // 2), 0)
    target = lax.broadcasted_iota(jnp.int32, (width, width // 2), 1)
    place = source - 2 * target + 1
    table = jnp.zeros((width, width // 2), jnp.float32)
    for p in range(4):
        table = table + pyramid_filter[p] * (place == p).astype(jnp.float32)
    return jnp.dot(values, table, precision=lax.Precision.HIGHEST)


def halve_rows(extended):
    pairs_count = extended.shape[2] // 2
    pairs = extended.reshape(extended.shape[:2] + (pairs_count, 2) + extended.shape[3:])
    even = pairs[:, :, :, 0]
    odd = pairs[:, :, :, 1]
    return (
        pyramid_filter[0] * even[:, :, :-1]
        + pyramid_filter[1] * odd[:, :, :-1]
        + pyramid_filter[2] * even[:, :, 1:]
        + pyramid_filter[3] * odd[:, :, 1:]
    )


def decimate_rim(extended):
    return halve_columns(halve_rows(extended))


def keep_rows(values, first, total):
    places = first + lax.iota(jnp.int32, values.shape[2])
    inside = (places >= 0) & (places < total)
    return jnp.where(inside[None, None, :, None], values, 0.0)


def smooth(level, clear):
    values = level.astype(jnp.float32)
    dates = values.shape[0]
    clear4 = clear[:, None]
    weight = 0.1 + 0.9 * clear4
    weighted = jnp.pad(weight * values, ((4, 4), (0, 0), (0, 0), (0, 0)))
    weight_pad = jnp.pad(weight, ((4, 4), (0, 0), (0, 0), (0, 0)))
    numer = jnp.zeros_like(values)
    denom = jnp.zeros_like(weight)
    for k in range(9):
        numer = numer + gap_weights[k] * weighted[k : k + dates]
        denom = denom + gap_weights[k] * weight_pad[k : k + dates]
    filled = clear4 * values + (1.0 - clear4) * (numer / denom)
    edged = jnp.pad(filled, ((4, 4), (0, 0), (0, 0), (0, 0)), mode="edge")
    result = jnp.zeros_like(values)
    for k in range(9):
        result = result + savgol_coeffs[k] * edged[k : k + dates]
    return result.astype(jnp.bfloat16)


def expand_mask(clear_mask, row_rep, col_rep):
    grown = jnp.repeat(jnp.repeat(clear_mask, row_rep, axis=1), col_rep, axis=2)
    return grown.astype(jnp.float32)


def local(scenes, resample_taps, clear_mask):
    rows = scenes.shape[2]
    extended = padded(scenes, (("row", 2),), 6)
    across = column_resample(extended, resample_taps[0])
    resampled_wide = valid_taps(across, resample_taps[1], 2)
    band_index = lax.axis_index("row")
    total_rows = rows * lax.axis_size("row")
    resampled_wide = keep_rows(resampled_wide, band_index * rows - 3, total_rows)
    half_wide = decimate_rim(resampled_wide)
    half_wide = keep_rows(half_wide, band_index * (rows // 2) - 1, total_rows // 2)
    resampled = resampled_wide[:, :, 3 : 3 + rows]
    half = half_wide[:, :, 1 : 1 + rows // 2]
    quarter = decimate_rim(half_wide)
    level_zero = resampled.astype(jnp.bfloat16)
    level_one = half.astype(jnp.bfloat16)
    level_two = quarter.astype(jnp.bfloat16)
    clear_fine = expand_mask(clear_mask, 4, 128)
    clear_half = expand_mask(clear_mask, 2, 64)
    clear_quarter = expand_mask(clear_mask, 1, 32)
    smooth_fine = smooth(
        lax.all_to_all(level_zero, "date", split_axis=2, concat_axis=0, tiled=True), clear_fine
    )
    smooth_half = smooth(
        lax.all_to_all(level_one, "date", split_axis=2, concat_axis=0, tiled=True), clear_half
    )
    smooth_quarter = smooth(
        lax.all_to_all(level_two, "date", split_axis=2, concat_axis=0, tiled=True), clear_quarter
    )
    return (smooth_fine, smooth_half, smooth_quarter)


def solution(mesh):
    in_specs = (P(("groups", "date"), None, "row", None), P(), P("groups", ("row", "date"), None))
    out_specs = (
        P("groups", None, ("row", "date"), None),
        P("groups", None, ("row", "date"), None),
        P("groups", None, ("row", "date"), None),
    )
    return jax.shard_map(local, mesh=mesh, in_specs=in_specs, out_specs=out_specs, check_vma=False)
```

profile of v0, /device:TPU:0, one launch (start us, length us, event | category | flops | bytes accessed | tf_op | source)
XLA Modules:
  0.0 176.9 jit_solution(12469758215546184341)
XLA Ops:
  0.6 0.9 fusion.313
  1.5 2.4 %collective-permute-start = (bf16[1,4,6,1024]{3,2,1,0:T(8,128)(2,1)S(1)}, bf16[1,4,6,1024]{3,2,1,0:T(8,128)(2,1)S(1)}, u32[]{:S(2)}, u32[]{:S(2)}) collective-permute-start(bf16[1,4,6,1024]{3,2,1,0:T(8,128)(2,1)S(1)} %get-tuple-element.21), channel_id=1, source_target_pairs={{0,1},{2,3},{4,5},{6,7},{8,9},{10,11},{12,13},{14,15},{16,17},{18,... | collective-permute-start | bytes 147464 | tf_op jit(solution)/shard_map/ppermute | solution.py:17
  3.9 1.3 collective-permute-start.1
  5.2 4.3 %fusion.83 = (f32[1024,1024]{1,0:T(8,128)}, f32[1024,1024]{1,0:T(8,128)}) fusion(), kind=kLoop, calls=%fused_computation.132 | loop fusion | flops 6291456 | bytes 8388608 | tf_op jit(solution)/shard_map/convert_element_type | solution.py:42
  9.5 4.3 %fusion.85 = (f32[1024,1024]{1,0:T(8,128)}, f32[1024,1024]{1,0:T(8,128)}) fusion(), kind=kLoop, calls=%fused_computation.134 | loop fusion | flops 6291456 | bytes 8388608 | tf_op jit(solution)/shard_map/convert_element_type | solution.py:42
  13.8 4.3 %fusion.87 = (f32[1024,1024]{1,0:T(8,128)}, f32[1024,1024]{1,0:T(8,128)}) fusion(), kind=kLoop, calls=%fused_computation.136 | loop fusion | flops 6291456 | bytes 8388608 | tf_op jit(solution)/shard_map/convert_element_type | solution.py:42
  18.2 2.5 %fusion.89 = f32[1024,1024]{1,0:T(8,128)} fusion(), kind=kLoop, calls=%fused_computation.138 | loop fusion | flops 4194304 | bytes 4194304 | tf_op jit(solution)/shard_map/convert_element_type | solution.py:42
  21.1 23.9 %fusion.96 = f32[1,4,268,1024]{3,2,1,0:T(8,128)S(1)} fusion(bf16[1,4,6,1024]{3,2,1,0:T(8,128)(2,1)S(1)} %collective-permute-done.1, bf16[1,4,256,1024]{3,2,1,0:T(8,128)(2,1)S(1)} %copy-done.1, bf16[1,4,6,1024]{3,2,1,0:T(8,128)(2,1)S(1)} %collective-permute-done, f32[1024,1024]{1,0:T(8,128)} %fusion.89, f32[4]{0:T(128)S(1)} %get-tuple-element.11, ...), kind=kOutput, calls=%fused_computation.152 | convolution fusion | flops 13549993984 | bytes 35946608 | tf_op jit(solution)/shard_map/tbrc,bcd->tbrd/dot_general | solution.py:43
  45.1 3.8 %fusion.29 = f32[1,4,262,1024]{3,2,1,0:T(8,128)S(1)} fusion(f32[1,4,268,1024]{3,2,1,0:T(8,128)S(1)} %fusion.96, f32[4]{0:T(128)S(1)} %get-tuple-element.42, f32[4]{0:T(128)S(1)} %get-tuple-element.41, f32[4]{0:T(128)S(1)} %get-tuple-element.40, f32[4]{0:T(128)S(1)} %get-tuple-element.39, f32[4]{0:T(128)S(1)} %get-tuple-element.38, ...), kind=kLoop, calls=%fused_computation.66 | loop fusion | flops 15024128 | bytes 34341240 | tf_op jit(solution)/shard_map/jit(_where)/select_n | solution.py:79
  48.9 2.8 %copy.24 = f32[1,4,262,1024]{3,1,2,0:T(4,128)S(1)} copy(f32[1,4,262,1024]{3,2,1,0:T(8,128)S(1)} %fusion.29) | data formatting | bytes 8585216 | tf_op jit(solution)/shard_map/jit(_where)/select_n | solution.py:79
  51.7 1.0 slice_bitcast_fusion.1
  52.7 2.3 %fusion.100 = f32[4,130,1024]{2,0,1:T(4,128)S(1)} fusion(f32[1,4,131,1024]{3,1,2,0:T(4,128)S(1)} %get-tuple-element.18, f32[1,4,131,1024]{3,1,2,0:T(4,128)S(1)} %get-tuple-element.17), kind=kLoop, calls=%fused_computation.157 | loop fusion | flops 3727360 | bytes 10649600 | tf_op jit(solution)/shard_map/reshape.35
  55.0 5.7 %fusion.119 = f32[4,130,512]{2,1,0:T(8,128)S(1)} fusion(f32[4,130,1024]{2,0,1:T(4,128)S(1)} %fusion.100, s32[512]{0:T(512)S(1)} %iota_multiply_fusion, pred[130]{0:T(512)(128)(4,1)S(1)} %compare_and_fusion), kind=kOutput, calls=%fused_computation.182 | convolution fusion | flops 3278639104 | bytes 3197058 | tf_op jit(solution)/shard_map/dot_general | solution.py:56
  61.9 0.9 fusion.124
  63.5 6.7 %all-to-all-start.2 = ((bf16[1,4,64,256]{3,1,0,2:T(4,128)(2,1)}), bf16[1,4,64,256]{3,1,0,2:T(4,128)(2,1)S(1)}, u32[]{:S(2)}, u32[]{:S(2)}) async-start(bf16[1,4,64,256]{3,1,0,2:T(4,128)(2,1)} %copy.32), calls=%async_computation.2 | async-start | bytes 262144 | tf_op jit(solution)/shard_map/all_to_all | solution.py:133
  70.4 1.2 copy.27
  71.6 6.8 %all-to-all-done.2 = bf16[1,4,64,256]{3,1,0,2:T(4,128)(2,1)S(1)} async-done(((bf16[1,4,64,256]{3,1,0,2:T(4,128)(2,1)}), bf16[1,4,64,256]{3,1,0,2:T(4,128)(2,1)S(1)}, u32[]{:S(2)}, u32[]{:S(2)}) %all-to-all-start.2) | async-done | bytes 131104 | tf_op jit(solution)/shard_map/all_to_all | solution.py:133
  78.4 3.5 %all-to-all-start.1 = ((bf16[1,4,128,512]{3,1,0,2:T(4,128)(2,1)}), bf16[1,4,128,512]{3,1,0,2:T(4,128)(2,1)S(1)}, u32[]{:S(2)}, u32[]{:S(2)}) async-start(bf16[1,4,128,512]{3,1,0,2:T(4,128)(2,1)} %copy.27), calls=%async_computation.1 | async-start | bytes 1048576 | tf_op jit(solution)/shard_map/all_to_all | solution.py:130
  82.2 2.8 %slice.1298 = bf16[1,4,256,1024]{3,2,1,0:T(8,128)(2,1)S(1)} slice(f32[1,4,262,1024]{3,2,1,0:T(8,128)} %copy-done), slice={[0:1], [0:4], [3:259], [0:1024]} | slice | bytes 4194304 | tf_op jit(solution)/shard_map/slice | solution.py:117
  85.0 2.9 %copy.22 = bf16[1,4,256,1024]{3,1,0,2:T(4,128)(2,1)} copy(bf16[1,4,256,1024]{3,2,1,0:T(8,128)(2,1)S(1)} %slice.1298) | data formatting | bytes 4194304 | tf_op jit(solution)/shard_map/slice | solution.py:117
  88.0 8.6 %all-to-all-done.1 = bf16[1,4,128,512]{3,1,0,2:T(4,128)(2,1)S(1)} async-done(((bf16[1,4,128,512]{3,1,0,2:T(4,128)(2,1)}), bf16[1,4,128,512]{3,1,0,2:T(4,128)(2,1)S(1)}, u32[]{:S(2)}, u32[]{:S(2)}) %all-to-all-start.1) | async-done | bytes 524320 | tf_op jit(solution)/shard_map/all_to_all | solution.py:130
  96.6 4.6 %all-to-all-start = ((bf16[1,4,256,1024]{3,1,0,2:T(4,128)(2,1)}), bf16[1,4,256,1024]{3,1,0,2:T(4,128)(2,1)}, u32[]{:S(2)}, u32[]{:S(2)}) async-start(bf16[1,4,256,1024]{3,1,0,2:T(4,128)(2,1)} %copy.22), calls=%async_computation | async-start | bytes 4194304 | tf_op jit(solution)/shard_map/all_to_all | solution.py:127
  102.8 1.3 broadcast_in_dim.78
  104.2 1.4 add.471
  105.8 1.4 fusion.155
  107.1 1.2 broadcast_subtract_fusion
  110.7 2.0 %fusion.129 = bf16[8,4,16,512]{3,2,1,0:T(8,128)(2,1)} fusion(f32[8,4,16,512]{3,2,1,0:T(8,128)S(1)} %fusion.182, f32[4,4,16,512]{3,2,1,0:T(8,128)S(1)} %reshape.284, f32[4,4,16,512]{3,2,1,0:T(8,128)S(1)} %reshape.283), kind=kLoop, calls=%fused_computation.205 | loop fusion | flops 6815744 | bytes 2621440 | tf_op jit(solution)/shard_map/convert_element_type | solution.py:99
  112.7 36.2 %all-to-all-done = bf16[1,4,256,1024]{3,1,0,2:T(4,128)(2,1)} async-done(((bf16[1,4,256,1024]{3,1,0,2:T(4,128)(2,1)}), bf16[1,4,256,1024]{3,1,0,2:T(4,128)(2,1)}, u32[]{:S(2)}, u32[]{:S(2)}) %all-to-all-start) | async-done | bytes 2097184 | tf_op jit(solution)/shard_map/all_to_all | solution.py:127
  149.0 2.8 %convert.18 = f32[1,4,8,32,1024]{4,1,3,2,0:T(4,128)S(1)} convert(bf16[1,4,8,32,1024]{4,1,3,2,0:T(4,128)(2,1)} %bitcast.43) | non-fusion elementwise | flops 1048576 | bytes 6291456 | tf_op jit(solution)/shard_map/convert_element_type | solution.py:83
  151.8 4.5 %bitcast_multiply_fusion = f32[8,4,32,1024]{3,2,1,0:T(8,128)} fusion(f32[1,4,8,32,1024]{4,1,3,2,0:T(4,128)S(1)} %convert.18, f32[8,32,1024]{2,1,0:T(8,128)S(1)} %get-tuple-element.28), kind=kLoop, calls=%fused_computation.121 | loop fusion | flops 1048576 | bytes 9437184 | tf_op jit(solution)/shard_map/mul | solution.py:87
  156.4 13.9 %fusion.75 = f32[8,4,32,1024]{3,2,1,0:T(8,128)S(1)} fusion(f32[8,4,32,1024]{3,2,1,0:T(8,128)} %bitcast_multiply_fusion, f32[1,4,8,32,1024]{4,1,3,2,0:T(4,128)S(1)} %convert.18, f32[8,32,1024]{2,1,0:T(8,128)} %fusion.155, f32[8,32,1024]{2,1,0:T(8,128)} %get-tuple-element.27, f32[8,32,1024]{2,1,0:T(8,128)S(1)} %convert_element_type.202), kind=kLoop, calls=%fused_computation.123 | loop fusion | flops 20971520 | bytes 15728640 | tf_op jit(solution)/shard_map/add | solution.py:94
  170.9 5.8 %fusion.39 = bf16[8,4,32,1024]{3,2,1,0:T(8,128)(2,1)} fusion(f32[8,4,32,1024]{3,2,1,0:T(8,128)S(1)} %fusion.75, f32[4,4,32,1024]{3,2,1,0:T(8,128)S(1)} %reshape.280, f32[4,4,32,1024]{3,2,1,0:T(8,128)S(1)} %reshape.279), kind=kLoop, calls=%fused_computation.82 | loop fusion | flops 27262976 | bytes 10485760 | tf_op jit(solution)/shard_map/convert_element_type | solution.py:99
  (62 shorter events, 7.4 us)
Async XLA Ops:
  1.5 19.6 %collective-permute-start = (bf16[1,4,6,1024]{3,2,1,0:T(8,128)(2,1)S(1)}, bf16[1,4,6,1024]{3,2,1,0:T(8,128)(2,1)S(1)}, u32[]{:S(2)}, u32[]{:S(2)}) collective-permute-start(bf16[1,4,6,1024]{3,2,1,0:T(8,128)(2,1)S(1)} %get-tuple-element.21), channel_id=1, source_target_pairs={{0,1},{2,3},{4,5},{6,7},{8,9},{10,11},{12,13},{14,15},{16,17},{18,... | collective-permute-start | bytes 147464 | tf_op jit(solution)/shard_map/ppermute | solution.py:17
  3.9 17.2 %collective-permute-start.1 = (bf16[1,4,6,1024]{3,2,1,0:T(8,128)(2,1)S(1)}, bf16[1,4,6,1024]{3,2,1,0:T(8,128)(2,1)S(1)}, u32[]{:S(2)}, u32[]{:S(2)}) collective-permute-start(bf16[1,4,6,1024]{3,2,1,0:T(8,128)(2,1)S(1)} %get-tuple-element.22), channel_id=1, source_target_pairs={{1,0},{3,2},{5,4},{7,6},{9,8},{11,10},{13,12},{15,14},{17,16},{19,... | collective-permute-start | bytes 147464 | tf_op jit(solution)/shard_map/ppermute | solution.py:20
  18.2 2.5 %copy-start.5 = (f32[2,4,7]{2,1,0:T(4,128)S(1)}, f32[2,4,7]{2,1,0:T(4,128)}, u32[]{:S(2)}) copy-start(f32[2,4,7]{2,1,0:T(4,128)} %param.4) | copy-start | bytes 676
  18.2 2.9 %copy-start.1 = (bf16[1,4,256,1024]{3,2,1,0:T(8,128)(2,1)S(1)}, bf16[1,4,256,1024]{3,2,1,0:T(8,128)(2,1)}, u32[]{:S(2)}) copy-start(bf16[1,4,256,1024]{3,2,1,0:T(8,128)(2,1)} %param.3) | copy-start | bytes 6291460
  48.9 2.8 %copy-start = (f32[1,4,262,1024]{3,2,1,0:T(8,128)}, f32[1,4,262,1024]{3,2,1,0:T(8,128)S(1)}, u32[]{:S(2)}) copy-start(f32[1,4,262,1024]{3,2,1,0:T(8,128)S(1)} %fusion.29) | copy-start | bytes 12877828
  61.9 20.0 %copy-start.4 = (s32[8,8,8]{2,1,0:T(8,128)S(1)}, s32[8,8,8]{2,1,0:T(8,128)}, u32[]{:S(2)}) copy-start(s32[8,8,8]{2,1,0:T(8,128)} %param.5) | copy-start | bytes 6148
  63.5 14.9 %all-to-all-start.2 = ((bf16[1,4,64,256]{3,1,0,2:T(4,128)(2,1)}), bf16[1,4,64,256]{3,1,0,2:T(4,128)(2,1)S(1)}, u32[]{:S(2)}, u32[]{:S(2)}) async-start(bf16[1,4,64,256]{3,1,0,2:T(4,128)(2,1)} %copy.32), calls=%async_computation.2 | async-start | bytes 262144 | tf_op jit(solution)/shard_map/all_to_all | solution.py:133
  78.4 9.6 %copy-start.2 = (bf16[1,4,64,256]{3,1,0,2:T(4,128)(2,1)}, bf16[1,4,64,256]{3,1,0,2:T(4,128)(2,1)S(1)}, u32[]{:S(2)}) copy-start(bf16[1,4,64,256]{3,1,0,2:T(4,128)(2,1)S(1)} %all-to-all-done.2) | copy-start | bytes 393220
  78.4 18.2 %all-to-all-start.1 = ((bf16[1,4,128,512]{3,1,0,2:T(4,128)(2,1)}), bf16[1,4,128,512]{3,1,0,2:T(4,128)(2,1)S(1)}, u32[]{:S(2)}, u32[]{:S(2)}) async-start(bf16[1,4,128,512]{3,1,0,2:T(4,128)(2,1)} %copy.27), calls=%async_computation.1 | async-start | bytes 1048576 | tf_op jit(solution)/shard_map/all_to_all | solution.py:130
  96.6 52.4 %all-to-all-start = ((bf16[1,4,256,1024]{3,1,0,2:T(4,128)(2,1)}), bf16[1,4,256,1024]{3,1,0,2:T(4,128)(2,1)}, u32[]{:S(2)}, u32[]{:S(2)}) async-start(bf16[1,4,256,1024]{3,1,0,2:T(4,128)(2,1)} %copy.22), calls=%async_computation | async-start | bytes 4194304 | tf_op jit(solution)/shard_map/all_to_all | solution.py:127
  104.2 4.2 %copy-start.3 = (bf16[1,4,64,256]{3,1,0,2:T(4,128)(2,1)S(1)}, bf16[1,4,64,256]{3,1,0,2:T(4,128)(2,1)}, u32[]{:S(2)}) copy-start(bf16[1,4,64,256]{3,1,0,2:T(4,128)(2,1)} %copy-done.2) | copy-start | bytes 393220
where the time goes:
time: 180 us; the launch traced here: 177 us
  other arithmetic  56 us (31%)
  waiting for transfers between devices  51.7 us (29%)
  matrix products  30.5 us (17%)
  local copies, waits for them, and re-layouts  19 us (11%)
  starting transfers between devices  18.4 us (10%)
    all_to_all x1, waiting for transfers between devices, local(): lax.all_to_all(level_zero, 'date', split_axis=2, concat_axis=0, tiled=True)  36.2 us
    dot_general x1, matrix products, column_resample(): jnp.einsum('tbrc,bcd->tbrd', values.astype(jnp.float32), table, precision...  23.9 us
    convert_element_type x4, other arithmetic, column_resample(): (offset == k).astype(jnp.float32)[None]  15.4 us
    add x3, other arithmetic, smooth(): filled = clear4 * values + (1.0 - clear4) * (numer / denom)  14.7 us
    convert_element_type x3, other arithmetic, smooth(): return result.astype(jnp.bfloat16)  8.65 us
    all_to_all x1, waiting for transfers between devices, local(): lax.all_to_all(level_one, 'date', split_axis=2, concat_axis=0, tiled=True)  8.64 us
    all_to_all x1, waiting for transfers between devices, local(): lax.all_to_all(level_two, 'date', split_axis=2, concat_axis=0, tiled=True)  6.81 us
    all_to_all x1, starting transfers between devices, local(): lax.all_to_all(level_two, 'date', split_axis=2, concat_axis=0, tiled=True)  6.67 us
  transfers between devices with their start and end apart: 5, of which 3 were waited for; matrix products, arithmetic and copies ran while one was open for 20% of the time, Pallas kernels for 0%

commit v1 on v0

--- a/solution.py
+++ b/solution.py
@@ -1,3 +1,4 @@
+import functools
 import math
 import jax
 import jax.numpy as jnp
@@ -7,6 +8,32 @@
 gap_weights = [math.exp(-((k - 4) ** 2) / 8.0) for k in range(9)]
 savgol_coeffs = [c / 231.0 for c in [-21.0, 14.0, 39.0, 54.0, 59.0, 54.0, 39.0, 14.0, -21.0]]
 pyramid_filter = [0.125, 0.375, 0.375, 0.125]
+
+
+def _pass_core(page, array_dim, dimension_no):
+    n_now = lax.axis_size("date")
+    mid_arr, arr_next = (n_now, lax.axis_index("date"))
+    wide_out = page.shape[array_dim] // mid_arr
+    y_new = list(page.shape)
+    y_new[array_dim] = wide_out
+    right_arr = y_new[dimension_no]
+    y_new[dimension_no] = right_arr * mid_arr
+    new = jnp.zeros(y_new, page.dtype)
+    for idx in range(mid_arr):
+        answer = lax.dynamic_slice_in_dim(
+            page, (arr_next ^ idx) * wide_out, wide_out, axis=array_dim
+        )
+        if idx:
+            answer = lax.ppermute(
+                answer, "date", [(dev_j, dev_j ^ idx) for dev_j in range(mid_arr)]
+            )
+        new = lax.dynamic_update_slice_in_dim(
+            new, answer, (arr_next ^ idx) * right_arr, axis=dimension_no
+        )
+    return new
+
+
+spread_target = functools.partial(_pass_core, array_dim=2, dimension_no=0)
 
 
 def padded(block, sides, width):
@@ -123,9 +150,7 @@
     clear_fine = expand_mask(clear_mask, 4, 128)
     clear_half = expand_mask(clear_mask, 2, 64)
     clear_quarter = expand_mask(clear_mask, 1, 32)
-    smooth_fine = smooth(
-        lax.all_to_all(level_zero, "date", split_axis=2, concat_axis=0, tiled=True), clear_fine
-    )
+    smooth_fine = smooth(spread_target(level_zero), clear_fine)
     smooth_half = smooth(
         lax.all_to_all(level_one, "date", split_axis=2, concat_axis=0, tiled=True), clear_half
     )

time: 180 us -> 168 us (0.933)
  the two profiles are of different devices: /device:TPU:0 before, /device:TPU:16 now
where the time goes in v1:
time: 168 us; the launch traced here: 167 us
  other arithmetic  47.3 us (28%)
  waiting for transfers between devices  43.4 us (26%)
  matrix products  30.9 us (18%)
  starting transfers between devices  23.2 us (14%)
  local copies, waits for them, and re-layouts  20.9 us (12%)
    ppermute x7, waiting for transfers between devices, _pass_core(): lax.ppermute(answer, 'date', [(dev_j, dev_j ^ idx) for dev_j in range(mid...  43.4 us
    dot_general x1, matrix products, column_resample(): jnp.einsum('tbrc,bcd->tbrd', values.astype(jnp.float32), table, precision...  24.4 us
    convert_element_type x4, other arithmetic, column_resample(): (offset == k).astype(jnp.float32)[None]  15.4 us
    convert_element_type x3, other arithmetic, smooth(): return result.astype(jnp.bfloat16)  8.52 us
    ppermute x7, starting transfers between devices, _pass_core(): lax.ppermute(answer, 'date', [(dev_j, dev_j ^ idx) for dev_j in range(mid...  8.35 us
    add x3, other arithmetic, smooth(): filled = clear4 * values + (1.0 - clear4) * (numer / denom)  6.97 us
    dot_general x2, matrix products, halve_columns(): return jnp.dot(values, table, precision=lax.Precision.HIGHEST)  6.56 us
    all_to_all x1, starting transfers between devices, local(): lax.all_to_all(level_two, 'date', split_axis=2, concat_axis=0, tiled=True)  6.17 us
  transfers between devices with their start and end apart: 11, of which 5 were waited for; matrix products, arithmetic and copies ran while one was open for 30% of the time, Pallas kernels for 0%

profile of v1, /device:TPU:16, one launch (start us, length us, event | category | flops | bytes accessed | tf_op | source)
XLA Modules:
  0.0 167.0 jit_solution(6161278882215309778)
XLA Ops:
  0.6 1.5 fusion.313
  2.2 2.4 %collective-permute-start = (bf16[1,4,6,1024]{3,2,1,0:T(8,128)(2,1)}, bf16[1,4,6,1024]{3,2,1,0:T(8,128)(2,1)}, u32[]{:S(2)}, u32[]{:S(2)}) collective-permute-start(bf16[1,4,6,1024]{3,2,1,0:T(8,128)(2,1)} %get-tuple-element.29), channel_id=1, source_target_pairs={{0,1},{2,3},{4,5},{6,7},{8,9},{10,11},{12,13},{14,15},{16,17},{18,... | collective-permute-start | bytes 147464 | tf_op jit(solution)/shard_map/ppermute | solution.py:44
  4.5 1.3 collective-permute-start.1
  5.8 4.3 %fusion.83 = (f32[1024,1024]{1,0:T(8,128)}, f32[1024,1024]{1,0:T(8,128)}) fusion(), kind=kLoop, calls=%fused_computation.132 | loop fusion | flops 6291456 | bytes 8388608 | tf_op jit(solution)/shard_map/convert_element_type | solution.py:69
  10.2 4.3 %fusion.85 = (f32[1024,1024]{1,0:T(8,128)}, f32[1024,1024]{1,0:T(8,128)}) fusion(), kind=kLoop, calls=%fused_computation.134 | loop fusion | flops 6291456 | bytes 8388608 | tf_op jit(solution)/shard_map/convert_element_type | solution.py:69
  14.4 4.3 %fusion.87 = (f32[1024,1024]{1,0:T(8,128)}, f32[1024,1024]{1,0:T(8,128)}) fusion(), kind=kLoop, calls=%fused_computation.136 | loop fusion | flops 6291456 | bytes 8388608 | tf_op jit(solution)/shard_map/convert_element_type | solution.py:69
  18.8 2.5 %fusion.89 = f32[1024,1024]{1,0:T(8,128)} fusion(), kind=kLoop, calls=%fused_computation.138 | loop fusion | flops 4194304 | bytes 4194304 | tf_op jit(solution)/shard_map/convert_element_type | solution.py:69
  26.7 1.7 %broadcast_subtract_fusion = (f32[8,32,1024]{2,1,0:T(8,128)}, f32[8,32,1024]{2,1,0:T(8,128)}) fusion(f32[8,32,1024]{2,1,0:T(8,128)S(1)} %convert_element_type.193), kind=kLoop, calls=%fused_computation.305 | loop fusion | flops 786432 | bytes 3145728 | tf_op jit(solution)/shard_map/sub | solution.py:121
  28.9 1.3 fusion.155
  30.7 24.4 %fusion.96 = f32[1,4,268,1024]{3,2,1,0:T(8,128)S(1)} fusion(bf16[1,4,6,1024]{3,2,1,0:T(8,128)(2,1)} %collective-permute-done.1, bf16[1,4,256,1024]{3,2,1,0:T(8,128)(2,1)} %param.3, bf16[1,4,6,1024]{3,2,1,0:T(8,128)(2,1)} %collective-permute-done, f32[1024,1024]{1,0:T(8,128)} %fusion.89, f32[4]{0:T(128)S(1)} %get-tuple-element.11, ...), kind=kOutput, calls=%fused_computation.152 | convolution fusion | flops 13549993984 | bytes 35946608 | tf_op jit(solution)/shard_map/tbrc,bcd->tbrd/dot_general | solution.py:70
  55.1 3.8 %fusion.29 = f32[1,4,262,1024]{3,2,1,0:T(8,128)S(1)} fusion(f32[1,4,268,1024]{3,2,1,0:T(8,128)S(1)} %fusion.96, f32[4]{0:T(128)S(1)} %get-tuple-element.50, f32[4]{0:T(128)S(1)} %get-tuple-element.49, f32[4]{0:T(128)S(1)} %get-tuple-element.48, f32[4]{0:T(128)S(1)} %get-tuple-element.47, f32[4]{0:T(128)S(1)} %get-tuple-element.46, ...), kind=kLoop, calls=%fused_computation.68 | loop fusion | flops 15024128 | bytes 34341240 | tf_op jit(solution)/shard_map/jit(_where)/select_n | solution.py:106
  58.9 2.8 %copy.20 = f32[1,4,262,1024]{3,1,2,0:T(4,128)S(1)} copy(f32[1,4,262,1024]{3,2,1,0:T(8,128)S(1)} %fusion.29) | data formatting | bytes 8585216 | tf_op jit(solution)/shard_map/jit(_where)/select_n | solution.py:106
  62.7 2.3 %fusion.100 = f32[4,130,1024]{2,0,1:T(4,128)S(1)} fusion(f32[1,4,131,1024]{3,1,2,0:T(4,128)S(1)} %get-tuple-element.18, f32[1,4,131,1024]{3,1,2,0:T(4,128)S(1)} %get-tuple-element.17), kind=kLoop, calls=%fused_computation.157 | loop fusion | flops 3727360 | bytes 10649600 | tf_op jit(solution)/shard_map/reshape.35
  65.1 5.7 %fusion.119 = f32[4,130,512]{2,1,0:T(8,128)S(1)} fusion(f32[4,130,1024]{2,0,1:T(4,128)S(1)} %fusion.100, s32[512]{0:T(512)S(1)} %iota_multiply_fusion, pred[130]{0:T(512)(128)(4,1)S(1)} %compare_and_fusion), kind=kOutput, calls=%fused_computation.182 | convolution fusion | flops 3278639104 | bytes 3197058 | tf_op jit(solution)/shard_map/dot_general | solution.py:83
  73.6 6.2 %all-to-all-start.1 = ((bf16[1,4,64,256]{3,1,0,2:T(4,128)(2,1)}), bf16[1,4,64,256]{3,1,0,2:T(4,128)(2,1)}, u32[]{:S(2)}, u32[]{:S(2)}) async-start(bf16[1,4,64,256]{3,1,0,2:T(4,128)(2,1)} %copy.28), calls=%async_computation.1 | async-start | bytes 262144 | tf_op jit(solution)/shard_map/all_to_all | solution.py:158
  79.8 2.8 %slice.1298 = bf16[1,4,256,1024]{3,2,1,0:T(8,128)(2,1)S(1)} slice(f32[1,4,262,1024]{3,2,1,0:T(8,128)} %copy-done), slice={[0:1], [0:4], [3:259], [0:1024]} | slice | bytes 4194304 | tf_op jit(solution)/shard_map/slice | solution.py:144
  82.8 1.2 copy.23
  84.3 1.3 constant_dynamic-slice_fusion
  85.5 1.5 collective-permute-start.2
  87.0 1.5 collective-permute-start.3
  89.0 3.8 %collective-permute-start.6 = (bf16[1,4,32,1024]{3,2,1,0:T(8,128)(2,1)}, bf16[1,4,32,1024]{3,2,1,0:T(8,128)(2,1)}, u32[]{:S(2)}, u32[]{:S(2)}) collective-permute-start(bf16[1,4,32,1024]{3,2,1,0:T(8,128)(2,1)} %get-tuple-element.23), channel_id=1, source_target_pairs={{0,10},{2,8},{4,14},{6,12},{8,2},{10,0},{12,6},{14,4},{1,11},{3,9}... | collective-permute-start | bytes 786440 | tf_op jit(solution)/shard_map/ppermute | solution.py:27
  92.9 5.1 %all-to-all-start = ((bf16[1,4,128,512]{3,1,0,2:T(4,128)(2,1)}), bf16[1,4,128,512]{3,1,0,2:T(4,128)(2,1)}, u32[]{:S(2)}, u32[]{:S(2)}) async-start(bf16[1,4,128,512]{3,1,0,2:T(4,128)(2,1)} %copy.23), calls=%async_computation | async-start | bytes 1048576 | tf_op jit(solution)/shard_map/all_to_all | solution.py:155
  98.0 1.0 convert.16
  102.4 2.0 %collective-permute-done.3 = bf16[1,4,32,1024]{3,2,1,0:T(8,128)(2,1)} collective-permute-done((bf16[1,4,32,1024]{3,2,1,0:T(8,128)(2,1)}, bf16[1,4,32,1024]{3,2,1,0:T(8,128)(2,1)}, u32[]{:S(2)}, u32[]{:S(2)}) %collective-permute-start.3) | collective-permute-done | bytes 262176 | tf_op jit(solution)/shard_map/ppermute | solution.py:27
  105.8 4.2 %collective-permute-done.4 = bf16[1,4,32,1024]{3,2,1,0:T(8,128)(2,1)} collective-permute-done((bf16[1,4,32,1024]{3,2,1,0:T(8,128)(2,1)}, bf16[1,4,32,1024]{3,2,1,0:T(8,128)(2,1)}, u32[]{:S(2)}, u32[]{:S(2)}) %collective-permute-start.4) | collective-permute-done | bytes 262176 | tf_op jit(solution)/shard_map/ppermute | solution.py:27
  112.0 1.5 collective-permute-done.6
  114.5 29.9 %collective-permute-done.7 = bf16[1,4,32,1024]{3,2,1,0:T(8,128)(2,1)S(1)} collective-permute-done((bf16[1,4,32,1024]{3,2,1,0:T(8,128)(2,1)}, bf16[1,4,32,1024]{3,2,1,0:T(8,128)(2,1)S(1)}, u32[]{:S(2)}, u32[]{:S(2)}) %collective-permute-start.7) | collective-permute-done | bytes 262176 | tf_op jit(solution)/shard_map/ppermute | solution.py:27
  144.4 5.8 %collective-permute-done.8 = bf16[1,4,32,1024]{3,2,1,0:T(8,128)(2,1)S(1)} collective-permute-done((bf16[1,4,32,1024]{3,2,1,0:T(8,128)(2,1)}, bf16[1,4,32,1024]{3,2,1,0:T(8,128)(2,1)S(1)}, u32[]{:S(2)}, u32[]{:S(2)}) %collective-permute-start.8) | collective-permute-done | bytes 262176 | tf_op jit(solution)/shard_map/ppermute | solution.py:27
  150.9 5.3 %fusion.35 = f32[8,4,32,1024]{3,2,1,0:T(8,128)S(1)} fusion(bf16[8,4,32,1024]{3,2,1,0:T(8,128)(2,1)S(1)} %constant_dynamic-update-slice_fusion, f32[8,4,32,1024]{3,2,1,0:T(8,128)S(1)} %convert_multiply_fusion, f32[8,32,1024]{2,1,0:T(8,128)} %fusion.155, f32[8,32,1024]{2,1,0:T(8,128)} %get-tuple-element.35, f32[8,32,1024]{2,1,0:T(8,128)S(1)} %convert_element_type.193), kind=kLoop, calls=%fused_computation.80 | loop fusion | flops 22020096 | bytes 13631488 | tf_op jit(solution)/shard_map/add | solution.py:121
  156.9 5.7 %fusion.40 = bf16[8,4,32,1024]{3,2,1,0:T(8,128)(2,1)} fusion(f32[8,4,32,1024]{3,2,1,0:T(8,128)S(1)} %fusion.35, f32[4,4,32,1024]{3,2,1,0:T(8,128)S(1)} %reshape.276, f32[4,4,32,1024]{3,2,1,0:T(8,128)S(1)} %reshape.275), kind=kLoop, calls=%fused_computation.85 | loop fusion | flops 27262976 | bytes 10485760 | tf_op jit(solution)/shard_map/convert_element_type | solution.py:126
  162.6 1.2 convert.15
  165.0 2.0 %fusion.129 = bf16[8,4,16,512]{3,2,1,0:T(8,128)(2,1)} fusion(f32[8,4,16,512]{3,2,1,0:T(8,128)S(1)} %fusion.182, f32[4,4,16,512]{3,2,1,0:T(8,128)S(1)} %reshape.280, f32[4,4,16,512]{3,2,1,0:T(8,128)S(1)} %reshape.279), kind=kLoop, calls=%fused_computation.205 | loop fusion | flops 6815744 | bytes 2621440 | tf_op jit(solution)/shard_map/convert_element_type | solution.py:126
  (85 shorter events, 21.3 us)
Async XLA Ops:
  2.2 28.5 %collective-permute-start = (bf16[1,4,6,1024]{3,2,1,0:T(8,128)(2,1)}, bf16[1,4,6,1024]{3,2,1,0:T(8,128)(2,1)}, u32[]{:S(2)}, u32[]{:S(2)}) collective-permute-start(bf16[1,4,6,1024]{3,2,1,0:T(8,128)(2,1)} %get-tuple-element.29), channel_id=1, source_target_pairs={{0,1},{2,3},{4,5},{6,7},{8,9},{10,11},{12,13},{14,15},{16,17},{18,... | collective-permute-start | bytes 147464 | tf_op jit(solution)/shard_map/ppermute | solution.py:44
  4.5 26.2 %collective-permute-start.1 = (bf16[1,4,6,1024]{3,2,1,0:T(8,128)(2,1)}, bf16[1,4,6,1024]{3,2,1,0:T(8,128)(2,1)}, u32[]{:S(2)}, u32[]{:S(2)}) collective-permute-start(bf16[1,4,6,1024]{3,2,1,0:T(8,128)(2,1)} %get-tuple-element.30), channel_id=1, source_target_pairs={{1,0},{3,2},{5,4},{7,6},{9,8},{11,10},{13,12},{15,14},{17,16},{19,... | collective-permute-start | bytes 147464 | tf_op jit(solution)/shard_map/ppermute | solution.py:47
  18.8 3.0 %copy-start.5 = (s32[8,8,8]{2,1,0:T(8,128)S(1)}, s32[8,8,8]{2,1,0:T(8,128)}, u32[]{:S(2)}) copy-start(s32[8,8,8]{2,1,0:T(8,128)} %param.5) | copy-start | bytes 6148
  18.8 3.1 %copy-start.6 = (f32[2,4,7]{2,1,0:T(4,128)S(1)}, f32[2,4,7]{2,1,0:T(4,128)}, u32[]{:S(2)}) copy-start(f32[2,4,7]{2,1,0:T(4,128)} %param.4) | copy-start | bytes 676
  58.9 2.8 %copy-start = (f32[1,4,262,1024]{3,2,1,0:T(8,128)}, f32[1,4,262,1024]{3,2,1,0:T(8,128)S(1)}, u32[]{:S(2)}) copy-start(f32[1,4,262,1024]{3,2,1,0:T(8,128)S(1)} %fusion.29) | copy-start | bytes 12877828
  70.7 1.2 copy-start.7
  73.6 19.3 %all-to-all-start.1 = ((bf16[1,4,64,256]{3,1,0,2:T(4,128)(2,1)}), bf16[1,4,64,256]{3,1,0,2:T(4,128)(2,1)}, u32[]{:S(2)}, u32[]{:S(2)}) async-start(bf16[1,4,64,256]{3,1,0,2:T(4,128)(2,1)} %copy.28), calls=%async_computation.1 | async-start | bytes 262144 | tf_op jit(solution)/shard_map/all_to_all | solution.py:158
  85.5 15.4 %collective-permute-start.2 = (bf16[1,4,32,1024]{3,2,1,0:T(8,128)(2,1)}, bf16[1,4,32,1024]{3,2,1,0:T(8,128)(2,1)}, u32[]{:S(2)}, u32[]{:S(2)}) collective-permute-start(bf16[1,4,32,1024]{3,2,1,0:T(8,128)(2,1)} %get-tuple-element.27), channel_id=1, source_target_pairs={{0,2},{2,0},{4,6},{6,4},{8,10},{10,8},{12,14},{14,12},{1,3},{3,1},... | collective-permute-start | bytes 786440 | tf_op jit(solution)/shard_map/ppermute | solution.py:27
  87.0 17.4 %collective-permute-start.3 = (bf16[1,4,32,1024]{3,2,1,0:T(8,128)(2,1)}, bf16[1,4,32,1024]{3,2,1,0:T(8,128)(2,1)}, u32[]{:S(2)}, u32[]{:S(2)}) collective-permute-start(bf16[1,4,32,1024]{3,2,1,0:T(8,128)(2,1)} %get-tuple-element.26), channel_id=1, source_target_pairs={{0,4},{2,6},{4,0},{6,2},{8,12},{10,14},{12,8},{14,10},{1,5},{3,7},... | collective-permute-start | bytes 786440 | tf_op jit(solution)/shard_map/ppermute | solution.py:27
  88.5 21.5 %collective-permute-start.4 = (bf16[1,4,32,1024]{3,2,1,0:T(8,128)(2,1)}, bf16[1,4,32,1024]{3,2,1,0:T(8,128)(2,1)}, u32[]{:S(2)}, u32[]{:S(2)}) collective-permute-start(bf16[1,4,32,1024]{3,2,1,0:T(8,128)(2,1)} %get-tuple-element.25), channel_id=1, source_target_pairs={{0,6},{2,4},{4,2},{6,0},{8,14},{10,12},{12,10},{14,8},{1,7},{3,5},... | collective-permute-start | bytes 786440 | tf_op jit(solution)/shard_map/ppermute | solution.py:27
  89.0 22.0 %collective-permute-start.5 = (bf16[1,4,32,1024]{3,2,1,0:T(8,128)(2,1)}, bf16[1,4,32,1024]{3,2,1,0:T(8,128)(2,1)}, u32[]{:S(2)}, u32[]{:S(2)}) collective-permute-start(bf16[1,4,32,1024]{3,2,1,0:T(8,128)(2,1)} %get-tuple-element.24), channel_id=1, source_target_pairs={{0,8},{2,10},{4,12},{6,14},{8,0},{10,2},{12,4},{14,6},{1,9},{3,11}... | collective-permute-start | bytes 786440 | tf_op jit(solution)/shard_map/ppermute | solution.py:27
  89.0 24.5 %collective-permute-start.6 = (bf16[1,4,32,1024]{3,2,1,0:T(8,128)(2,1)}, bf16[1,4,32,1024]{3,2,1,0:T(8,128)(2,1)}, u32[]{:S(2)}, u32[]{:S(2)}) collective-permute-start(bf16[1,4,32,1024]{3,2,1,0:T(8,128)(2,1)} %get-tuple-element.23), channel_id=1, source_target_pairs={{0,10},{2,8},{4,14},{6,12},{8,2},{10,0},{12,6},{14,4},{1,11},{3,9}... | collective-permute-start | bytes 786440 | tf_op jit(solution)/shard_map/ppermute | solution.py:27
  92.9 69.8 %all-to-all-start = ((bf16[1,4,128,512]{3,1,0,2:T(4,128)(2,1)}), bf16[1,4,128,512]{3,1,0,2:T(4,128)(2,1)}, u32[]{:S(2)}, u32[]{:S(2)}) async-start(bf16[1,4,128,512]{3,1,0,2:T(4,128)(2,1)} %copy.23), calls=%async_computation | async-start | bytes 1048576 | tf_op jit(solution)/shard_map/all_to_all | solution.py:155
  98.0 52.3 %copy-start.1 = (f32[8,32,1024]{2,1,0:T(8,128)S(1)}, f32[8,32,1024]{2,1,0:T(8,128)}, u32[]{:S(2)}) copy-start(f32[8,32,1024]{2,1,0:T(8,128)} %get-tuple-element.36) | copy-start | bytes 3145732
  100.9 43.4 %collective-permute-start.7 = (bf16[1,4,32,1024]{3,2,1,0:T(8,128)(2,1)}, bf16[1,4,32,1024]{3,2,1,0:T(8,128)(2,1)S(1)}, u32[]{:S(2)}, u32[]{:S(2)}) collective-permute-start(bf16[1,4,32,1024]{3,2,1,0:T(8,128)(2,1)} %get-tuple-element.22), channel_id=1, source_target_pairs={{0,12},{2,14},{4,8},{6,10},{8,4},{10,6},{12,0},{14,2},{1,13},{3,15... | collective-permute-start | bytes 786440 | tf_op jit(solution)/shard_map/ppermute | solution.py:27
  104.4 45.8 %collective-permute-start.8 = (bf16[1,4,32,1024]{3,2,1,0:T(8,128)(2,1)}, bf16[1,4,32,1024]{3,2,1,0:T(8,128)(2,1)S(1)}, u32[]{:S(2)}, u32[]{:S(2)}) collective-permute-start(bf16[1,4,32,1024]{3,2,1,0:T(8,128)(2,1)} %get-tuple-element.21), channel_id=1, source_target_pairs={{0,14},{2,12},{4,10},{6,8},{8,6},{10,4},{12,2},{14,0},{1,15},{3,13... | collective-permute-start | bytes 786440 | tf_op jit(solution)/shard_map/ppermute | solution.py:27
  156.9 6.9 %copy-start.2 = (f32[8,16,512]{2,1,0:T(8,128)S(1)}, f32[8,16,512]{2,1,0:T(8,128)}, u32[]{:S(2)}) copy-start(f32[8,16,512]{2,1,0:T(8,128)} %get-tuple-element.40) | copy-start | bytes 786436
  156.9 7.3 %copy-start.3 = (f32[8,16,512]{2,1,0:T(8,128)S(1)}, f32[8,16,512]{2,1,0:T(8,128)}, u32[]{:S(2)}) copy-start(f32[8,16,512]{2,1,0:T(8,128)} %get-tuple-element.39) | copy-start | bytes 786436
  156.9 7.3 %copy-start.4 = (f32[8,16,512]{2,1,0:T(8,128)S(1)}, f32[8,16,512]{2,1,0:T(8,128)}, u32[]{:S(2)}) copy-start(f32[8,16,512]{2,1,0:T(8,128)} %fusion.242) | copy-start | bytes 786436
